TPU v7x, 32 devices: a whole 2x2x4 slice. The times are simulated.
32 devices in a mesh: groups: 2 (over x), chan: 16 (over z, y, core), freq: 1.
Axes of the slice: x: 2, y: 2, z: 4, core: 2. Of those that a mesh axis runs over, the one named last changes fastest.
Arguments:
- raw: bfloat16 [256, 16, 12000], P(('groups', 'chan'), 'freq'), parts along dimension 0, may hold values from -100 to 100, as said below
- lengths: int32 [256, 16], P(('groups', 'chan'), 'freq'), parts along dimension 0, may hold values from 6000 to 12000
- quality: int32 [256], P('groups'), parts along dimension 0, may hold values 0 or 1
- assignment: int32 [256], P('groups'), parts along dimension 0, may hold values from 0 to 127, as said below
Outputs:
- cross: bfloat16 [512, 256, 2, 128], P('freq', ('groups', 'chan')), parts along dimension 1
There are 2 independent parts, one for each index of `groups`. A program takes and returns all parts, laid end to end along the dimension named above; each array names one. Nothing has to cross between parts.
Inputs may be any that keep to these rules, and one draw needn't show every extreme that they name: `raw`: records are clipped to this range. `assignment`: A permutation. The 8 channels of one file block (consecutive entries) land at most 1 in any one block of 8 consecutive positions, and some pair of blocks reaches 1.
All inputs are finite; a program needn't handle non-finite values.
Results may differ from a plain program's by a relative error of at most 0.012.
The roundings to bfloat16 on the way count: a program that leaves them out, or rounds other values in their place, can miss the bound.
Values may be sent and summed in bfloat16 or wider, within the bound.
No kernel may reach another device: no remote copies, remote signals or barrier semaphores. Data moves between devices by JAX's collectives and lax.ppermute only.
A program may use at most 128 MiB of HBM per device.

v0:
```python
import math
import jax
import jax.numpy as jnp
from jax import lax
from jax.sharding import PartitionSpec as P

WIN = 12000
NB = 512
K0 = 6
SUB = 32


def dft_table(first_sample, sample_count):
    samples = first_sample + jnp.arange(sample_count, dtype=jnp.int32)
    bin_index = K0 + jnp.arange(NB, dtype=jnp.int32)
    residue = samples[:, None] * bin_index[None, :] % WIN
    angles = residue.astype(jnp.float32) * (2.0 * math.pi / WIN)
    return jnp.concatenate([jnp.cos(angles), -jnp.sin(angles)], axis=1).astype(jnp.bfloat16)


def prepare(raw_block, valid_lengths):
    positions = jnp.arange(WIN, dtype=jnp.int32)
    inside = positions[None, None, :] < valid_lengths[:, :, None]
    values = raw_block.astype(jnp.float32)
    kept = jnp.where(inside, values, 0.0)
    average = jnp.sum(kept, axis=-1) / valid_lengths.astype(jnp.float32)
    taper = 0.5 - 0.5 * jnp.cos(positions.astype(jnp.float32) * (2.0 * math.pi / WIN))
    return jnp.where(inside, (values - average[:, :, None]) * taper[None, None, :], 0.0).astype(
        jnp.bfloat16
    )


def whiten(spectra):
    row_count = spectra.shape[0]
    grouped = spectra.reshape(row_count, 2, NB // SUB, SUB)
    power = jnp.sum(grouped * grouped, axis=(1, 3)) / SUB
    factor = lax.rsqrt(power + 1e-06)
    return (grouped * factor[:, None, :, None]).reshape(row_count, 2, NB).astype(jnp.bfloat16)


def spectra_of(shaped_rows):
    row_count = shaped_rows.shape[0]
    pieces = 8
    block_width = WIN // pieces
    total = jnp.zeros((row_count, 2 * NB), jnp.float32)
    for block_index in range(pieces):
        first_sample = block_index * block_width
        segment = lax.slice_in_dim(shaped_rows, first_sample, first_sample + block_width, axis=1)
        total = total + jnp.dot(
            segment, dft_table(first_sample, block_width), preferred_element_type=jnp.float32
        )
    return whiten(total)


def cross_block(left_rows, right_rows, all_windows):
    bins_here = left_rows.shape[3]
    left_side = left_rows.transpose(3, 0, 2, 1).reshape(
        bins_here, left_rows.shape[0], 2 * all_windows
    )
    right_count = right_rows.shape[0]
    right_plain = right_rows.transpose(3, 2, 1, 0).reshape(bins_here, 2 * all_windows, right_count)
    turned = jnp.stack([-right_rows[:, :, 1], right_rows[:, :, 0]], axis=2)
    right_turned = turned.transpose(3, 2, 1, 0).reshape(bins_here, 2 * all_windows, right_count)
    real_part = jnp.einsum(
        "bik,bkj->bij", left_side, right_plain, preferred_element_type=jnp.float32
    )
    imag_part = jnp.einsum(
        "bik,bkj->bij", left_side, right_turned, preferred_element_type=jnp.float32
    )
    return (jnp.stack([real_part, imag_part], axis=2) / all_windows).astype(jnp.bfloat16)


def body(raw, lengths, quality, assignment):
    channel_count = lax.axis_size("chan")
    my_index = lax.axis_index("chan")
    block_rows, window_count, sample_count = raw.shape
    capacity = max(1, block_rows // channel_count)
    total_channels = assignment.shape[0]
    targets_all = assignment.reshape(channel_count, block_rows) // block_rows
    row_numbers = jnp.arange(block_rows, dtype=jnp.int32)
    same_target = targets_all[:, :, None] == targets_all[:, None, :]
    earlier = row_numbers[None, None, :] < row_numbers[None, :, None]
    slot_table = jnp.sum(jnp.logical_and(same_target, earlier), axis=2)
    quality_table = quality.reshape(channel_count, block_rows)
    my_targets = lax.dynamic_index_in_dim(targets_all, my_index, 0, keepdims=False)
    my_slots = lax.dynamic_index_in_dim(slot_table, my_index, 0, keepdims=False)
    my_quality = lax.dynamic_index_in_dim(quality_table, my_index, 0, keepdims=False)
    device_numbers = jnp.arange(channel_count, dtype=jnp.int32)
    slot_numbers = jnp.arange(capacity, dtype=jnp.int32)
    match_table = jnp.logical_and(
        jnp.logical_and(
            my_targets[None, None, :] == device_numbers[:, None, None],
            my_slots[None, None, :] == slot_numbers[None, :, None],
        ),
        my_quality[None, None, :] == 1,
    )
    present = jnp.any(match_table, axis=2).reshape(-1)
    source_row = jnp.sum(jnp.where(match_table, row_numbers[None, None, :], 0), axis=2).reshape(-1)
    inverse = (
        jnp.zeros((total_channels,), jnp.int32)
        .at[assignment]
        .set(jnp.arange(total_channels, dtype=jnp.int32))
    )
    arrivals = lax.dynamic_slice_in_dim(inverse, my_index * block_rows, block_rows)
    source_device = arrivals // block_rows
    flat_slot = source_device * capacity + jnp.take(slot_table.reshape(-1), arrivals)
    arrival_good = jnp.take(quality, arrivals)
    shaped = prepare(raw, lengths)
    picked = jnp.take(shaped, source_row, axis=0)
    kept_rows = picked * present.astype(shaped.dtype).reshape((-1,) + (1,) * (shaped.ndim - 1))
    arrived = lax.all_to_all(
        kept_rows.reshape((channel_count, capacity) + shaped.shape[1:]),
        "chan",
        split_axis=0,
        concat_axis=0,
        tiled=True,
    )
    flat_rows = arrived.reshape((channel_count * capacity,) + arrived.shape[2:])
    picked = jnp.take(flat_rows, flat_slot, axis=0)
    local_rows = picked * arrival_good.astype(arrived.dtype).reshape(
        (-1,) + (1,) * (arrived.ndim - 2)
    )
    whitened = spectra_of(local_rows.reshape(block_rows * window_count, sample_count)).reshape(
        block_rows, window_count, 2, NB
    )
    panel = lax.all_to_all(whitened, "freq", split_axis=3, concat_axis=1, tiled=True)
    all_windows = panel.shape[1]
    return cross_block(panel, lax.all_gather(panel, "chan", axis=0, tiled=True), all_windows)


def solution(mesh):
    return jax.shard_map(
        body,
        mesh=mesh,
        in_specs=(
            P(("groups", "chan"), "freq", None),
            P(("groups", "chan"), "freq"),
            P("groups"),
            P("groups"),
        ),
        out_specs=P("freq", ("groups", "chan"), None, None),
        check_vma=False,
    )
```

profile of v0, /device:TPU:0, one launch (start us, length us, event | category | flops | bytes accessed | tf_op | source)
XLA Modules:
  0.0 277.0 jit_solution(14290823064365634316)
XLA Ops:
  6.5 0.7 reshape.391
  7.3 0.7 reshape.389
  8.8 3.3 %fusion = f32[8,16]{1,0:T(8,128)S(1)} fusion(bf16[8,16,12000]{2,1,0:T(8,128)(2,1)} %param.6, s32[8,16]{1,0:T(8,128)} %param.7), kind=kLoop, calls=%fused_computation.7 | loop fusion | flops 6143872 | bytes 3073024 | tf_op jit(solution)/shard_map/reduce_sum | solution.py:26
  12.1 1.5 fusion.3
  13.6 3.5 %gather_fusion = bf16[16,16,12000]{2,1,0:T(8,128)(2,1)} fusion(bf16[8,16,12000]{2,1,0:T(8,128)(2,1)S(1)} %fusion.3, s32[1024]{0:T(1024)S(1)} %pad_clamp_fusion.1), kind=kCustom, calls=%fused_computation.2 | custom fusion | bytes 12288064 | tf_op jit(solution)/shard_map/jit(_take)/gather | solution.py:109
  17.2 6.0 %fusion.4 = bf16[16,1,16,12000]{3,2,1,0:T(8,128)(2,1)} fusion(bf16[16,16,12000]{2,1,0:T(8,128)(2,1)} %gather_fusion, pred[16]{0:T(512)(128)(4,1)S(1)} %compare_and_fusion.1, bf16[16]{0:T(256)(128)(2,1)S(1)} %convert_element_type.89), kind=kLoop, calls=%fused_computation.12 | loop fusion | flops 6144000 | bytes 12288048 | tf_op jit(solution)/shard_map/mul | solution.py:110
  23.1 7.6 %all-to-all-start = ((bf16[16,1,16,12000]{3,2,1,0:T(8,128)(2,1)}), bf16[16,1,16,12000]{3,2,1,0:T(8,128)(2,1)}, u32[]{:S(2)}, u32[]{:S(2)}) async-start(bf16[16,1,16,12000]{3,2,1,0:T(8,128)(2,1)} %fusion.4), calls=%async_computation | async-start | bytes 12320768 | tf_op jit(solution)/shard_map/all_to_all | solution.py:111
  30.9 1.2 scatter_custom_fusion
  32.1 0.6 gather_fusion.3
  33.1 0.6 gather_fusion.2
  34.1 109.5 %cosine_convert_fusion = (bf16[1500,512]{1,0:T(8,128)(2,1)}, bf16[1500,512]{1,0:T(8,128)(2,1)}, bf16[1500,512]{1,0:T(8,128)(2,1)}, bf16[1500,512]{1,0:T(8,128)(2...) fusion(s32[1500]{0:T(1024)S(1)} %get-tuple-element.40, ...), kind=kLoop, calls=%fused_computation.76 | loop fusion | flops 73728000 | bytes 24620048 | tf_op jit(solution)/shard_map/convert
  143.6 3.5 %gather_fusion.1 = bf16[8,16,12000]{2,1,0:T(8,128)(2,1)S(1)} fusion(bf16[16,16,12000]{2,1,0:T(8,128)(2,1)} %bitcast.5, s32[1024]{0:T(1024)S(1)} %pad_clamp_fusion), kind=kCustom, calls=%fused_computation.3 | custom fusion | bytes 6144032 | tf_op jit(solution)/shard_map/jit(_take)/gather | solution.py:119
  147.6 0.9 copy-done.17
  149.5 0.8 copy-done.15
  150.8 0.6 fusion.97
  151.5 0.8 copy-done.13
  153.3 0.8 copy-done.11
  155.2 0.8 copy-done.9
  157.0 0.8 copy-done.7
  158.9 0.8 copy-done.5
  160.8 0.8 copy-done.3
  162.0 0.6 fusion.127
  164.2 0.8 fusion.100
  165.0 1.7 copy.42
  166.8 70.6 %all-gather.2.cloned.1.call-done = bf16[128,16,2,512]{3,1,2,0:T(8,128)(2,1)} async-done(((bf16[8,16,2,512]{3,1,2,0:T(8,128)(2,1)}), bf16[128,16,2,512]{3,1,2,0:T(8,128)(2,1)}) %all-gather.2.cloned.1.call-update) | async-done | bytes 4194320 | tf_op jit(solution)/shard_map/all_gather | solution.py:128
  237.4 9.1 %copy.41 = bf16[512,2,16,128]{3,2,1,0:T(8,128)(2,1)} copy(bf16[512,2,16,128]{0,2,1,3:T(8,128)(2,1)} %bitcast.37) | data formatting | bytes 8388608 | tf_op jit(solution)/shard_map/transpose | solution.py:61
  246.5 2.5 slice_negate_fusion
  249.0 2.3 maximum_bitcast_fusion
  251.3 9.1 %copy.43 = bf16[512,2,16,128]{3,2,1,0:T(8,128)(2,1)} copy(bf16[512,2,16,128]{0,2,1,3:T(8,128)(2,1)} %maximum_bitcast_fusion) | data formatting | bytes 8388608 | tf_op jit(solution)/shard_map/transpose | solution.py:63
  260.5 3.5 %convolution_bitcast_fusion.1 = f32[512,8,1,128]{3,1,0,2:T(8,128)S(1)} fusion(bf16[512,8,32]{2,1,0:T(8,128)(2,1)S(1)} %copy.42, bf16[512,32,128]{2,1,0:T(8,128)(2,1)} %bitcast.35), kind=kOutput, calls=%fused_computation.125 | convolution fusion | flops 33554432 | bytes 6553600 | tf_op jit(solution)/shard_map/bik,bkj->bij/dot_general | solution.py:64
  264.0 1.3 convolution_bitcast_fusion
  265.6 4.6 %copy.45 = bf16[512,8,2,128]{3,2,1,0:T(2,128)(2,1)} copy(bf16[512,8,2,128]{3,1,0,2:T(8,128)(2,1)S(1)} %fusion.5) | data formatting | bytes 4194304 | tf_op jit(solution)/shard_map/convert_element_type | solution.py:70
  (85 shorter events, 11.5 us)
Async XLA Ops:
  6.5 5.5 %copy-start.19 = (s32[8,16]{1,0:T(8,128)S(1)}, s32[8,16]{1,0:T(8,128)}, u32[]{:S(2)}) copy-start(s32[8,16]{1,0:T(8,128)} %param.7) | copy-start | bytes 1540
  8.1 4.0 %copy-start.2 = (bf16[8,16,12000]{2,1,0:T(8,128)(2,1)S(1)}, bf16[8,16,12000]{2,1,0:T(8,128)(2,1)}, u32[]{:S(2)}) copy-start(bf16[8,16,12000]{2,1,0:T(8,128)(2,1)} %param.6) | copy-start | bytes 9216004
  23.1 7.7 %copy-start.20 = (s32[128]{0:T(128)S(1)}, s32[128]{0:T(128)}, u32[]{:S(2)}) copy-start(s32[128]{0:T(128)} %param.9) | copy-start | bytes 1540
  23.1 9.0 %copy-start = (s32[128]{0:T(128)S(1)}, s32[128]{0:T(128)}, u32[]{:S(2)}) copy-start(s32[128]{0:T(128)} %param.8) | copy-start | bytes 1540
  23.1 120.5 %all-to-all-start = ((bf16[16,1,16,12000]{3,2,1,0:T(8,128)(2,1)}), bf16[16,1,16,12000]{3,2,1,0:T(8,128)(2,1)}, u32[]{:S(2)}, u32[]{:S(2)}) async-start(bf16[16,1,16,12000]{3,2,1,0:T(8,128)(2,1)} %fusion.4), calls=%async_computation | async-start | bytes 12320768 | tf_op jit(solution)/shard_map/all_to_all | solution.py:111
  30.7 206.6 %all-gather.2.cloned.1.call-start = ((), (), s32[]{:S(2)}) async-start(), calls=%async_computation.1 | async-start | bytes 4456448 | tf_op jit(solution)/shard_map/all_gather | solution.py:128
  147.1 1.4 copy-start.17
  147.1 1.9 copy-start.18
  149.0 1.4 copy-start.15
  149.0 1.9 copy-start.16
  150.8 1.4 copy-start.13
  150.8 1.9 copy-start.14
  152.7 1.4 copy-start.11
  152.7 1.9 copy-start.12
  154.5 1.4 copy-start.9
  154.5 1.9 copy-start.10
  156.4 1.4 copy-start.7
  156.4 1.9 copy-start.8
  158.3 1.4 copy-start.5
  158.3 1.9 copy-start.6
  160.1 1.4 copy-start.3
  160.1 1.9 copy-start.4
  260.5 3.5 %copy-start.1 = (bf16[512,2,16,128]{3,2,1,0:T(8,128)(2,1)S(1)}, bf16[512,2,16,128]{3,2,1,0:T(8,128)(2,1)}, u32[]{:S(2)}) copy-start(bf16[512,2,16,128]{3,2,1,0:T(8,128)(2,1)} %copy.43) | copy-start | bytes 12582916
Sparse Core Ops, SparseCore 0:
  165.1 72.1 all-gather.1
where the time goes:
time: 278 us; the launch traced here: 277 us
  other arithmetic  128 us (46%)
  waiting for transfers between devices  70.6 us (25%)
  local copies, waits for them, and re-layouts  47.6 us (17%)
  between operations  13.7 us (5%)
  matrix products  9.73 us (4%)
  starting transfers between devices  7.63 us (3%)
    another operation x1, other arithmetic  110 us
    all_gather x1, waiting for transfers between devices, body(): lax.all_gather(panel, 'chan', axis=0, tiled=True)  70.6 us
    unnamed x42, local copies, waits for them, and re-layouts  10 us
    transpose x1, local copies, waits for them, and re-layouts, cross_block(): turned.transpose(3, 2, 1, 0)  9.15 us
    transpose x1, local copies, waits for them, and re-layouts, cross_block(): right_rows.transpose(3, 2, 1, 0)  9.12 us
    all_to_all x1, starting transfers between devices, body(): lax.all_to_all(kept_rows.reshape((channel_count, capacity) + shaped.shape...  7.59 us
    mul x1, other arithmetic, body(): picked * present.astype(shaped.dtype).reshape((-1,) + (1,) * (shaped.ndim...  5.97 us
  transfers between devices with their start and end apart: 2, of which 1 were waited for; matrix products, arithmetic and copies ran while one was open for 41% of the time, Pallas kernels for 0%

commit v1 on v0

--- a/solution.py
+++ b/solution.py
@@ -108,13 +108,20 @@
     shaped = prepare(raw, lengths)
     picked = jnp.take(shaped, source_row, axis=0)
     kept_rows = picked * present.astype(shaped.dtype).reshape((-1,) + (1,) * (shaped.ndim - 1))
-    arrived = lax.all_to_all(
-        kept_rows.reshape((channel_count, capacity) + shaped.shape[1:]),
-        "chan",
-        split_axis=0,
-        concat_axis=0,
-        tiled=True,
-    )
+    x = kept_rows.reshape((channel_count, capacity) + shaped.shape[1:])
+    ways, here = (lax.axis_size("chan"), lax.axis_index("chan"))
+    width = x.shape[0] // ways
+    dims = list(x.shape)
+    dims[0] = width
+    height = dims[0]
+    dims[0] = height * ways
+    full = jnp.zeros(dims, x.dtype)
+    for mask in range(ways):
+        part = lax.dynamic_slice_in_dim(x, (here ^ mask) * width, width, axis=0)
+        if mask:
+            part = lax.ppermute(part, "chan", [(d, d ^ mask) for d in range(ways)])
+        full = lax.dynamic_update_slice_in_dim(full, part, (here ^ mask) * height, axis=0)
+    arrived = full
     flat_rows = arrived.reshape((channel_count * capacity,) + arrived.shape[2:])
     picked = jnp.take(flat_rows, flat_slot, axis=0)
     local_rows = picked * arrival_good.astype(arrived.dtype).reshape(

time: 278 us -> 412 us (1.48)
  waiting for transfers between devices: 70.6 us -> 180 us
  local copies, waits for them, and re-layouts: 47.6 us -> 64.4 us
  starting transfers between devices: 7.63 us -> 16.8 us
    ppermute x0 -> x15, waiting for transfers between devices: none -> 133 us  [body(): part = lax.ppermute(part, 'chan', [(d, d ^ mask) for d in range(ways)])]
    all_gather x1, waiting for transfers between devices: 70.6 us -> 47.2 us  [body(): lax.all_gather(panel, 'chan', axis=0, tiled=True)]
    ppermute x0 -> x15, starting transfers between devices: none -> 16.8 us  [body(): part = lax.ppermute(part, 'chan', [(d, d ^ mask) for d in range(ways)])]
    dynamic_update_slice x0 -> x15, local copies, waits for them, and re-layouts: none -> 11.7 us  [body(): lax.dynamic_update_slice_in_dim(full, part, (here ^ mask) * height, axis=0)]
    all_to_all x1 -> x0, starting transfers between devices: 7.59 us -> none  [body(): lax.all_to_all(kept_rows.reshape((channel_count, capacity) + shaped.shape...]
    unnamed x42 -> x54, local copies, waits for them, and re-layouts: 10 us -> 12.6 us
  transfers between devices with their start and end apart: 2 -> 16, of which waited for: 1 -> 11; matrix products, arithmetic and copies ran while one was open for 41% -> 30% of each run, Pallas kernels for 0% -> 0%
where the time goes in v1:
time: 412 us; the launch traced here: 411 us
  waiting for transfers between devices  180 us (44%)
  other arithmetic  127 us (31%)
  local copies, waits for them, and re-layouts  64.4 us (16%)
  starting transfers between devices  16.8 us (4%)
  between operations  13.9 us (3%)
  matrix products  9.73 us (2%)
    ppermute x15, waiting for transfers between devices, body(): part = lax.ppermute(part, 'chan', [(d, d ^ mask) for d in range(ways)])  133 us
    another operation x1, other arithmetic  109 us
    all_gather x1, waiting for transfers between devices, body(): lax.all_gather(panel, 'chan', axis=0, tiled=True)  47.2 us
    ppermute x15, starting transfers between devices, body(): part = lax.ppermute(part, 'chan', [(d, d ^ mask) for d in range(ways)])  16.8 us
    unnamed x54, local copies, waits for them, and re-layouts  12.6 us
    dynamic_update_slice x15, local copies, waits for them, and re-layouts, body(): lax.dynamic_update_slice_in_dim(full, part, (here ^ mask) * height, axis=0)  11.7 us
    transpose x1, local copies, waits for them, and re-layouts, cross_block(): turned.transpose(3, 2, 1, 0)  9.14 us
    transpose x1, local copies, waits for them, and re-layouts, cross_block(): right_rows.transpose(3, 2, 1, 0)  9.14 us
  transfers between devices with their start and end apart: 16, of which 11 were waited for; matrix products, arithmetic and copies ran while one was open for 30% of the time, Pallas kernels for 0%

profile of v1, /device:TPU:0, one launch (start us, length us, event | category | flops | bytes accessed | tf_op | source)
XLA Modules:
  0.0 411.3 jit_solution(5913103284761975053)
XLA Ops:
  8.8 3.0 fusion
  12.0 3.3 fusion.3
  15.3 3.6 gather_fusion
  18.9 3.4 select_multiply_fusion
  22.7 2.0 dynamic-slice_bitcast_fusion
  24.7 2.6 copy-done.2
  27.3 5.5 %collective-permute-start.14 = (bf16[1,1,16,12000]{3,2,1,0:T(8,128)(2,1)S(1)}, bf16[1,1,16,12000]{3,2,1,0:T(8,128)(2,1)S(1)}, u32[]{:S(2)}, u32[]{:S(2)}) collective-permute-start(bf16[1,1,16,12000]{3,2,1,0:T(8,128)(2,1)S(1)} %get-tuple-element.8), channel_id=1, source_target_pairs={{0,15},{1,14},{2,13},{3,12},{4,11},{5,10},{6,9},{7,8},{8,7},{9,6},... | collective-permute-start | bytes 1152008 | tf_op jit(solution)/shard_map/ppermute | solution.py:122
  33.4 3.2 collective-permute-start.12
  39.0 109.5 %cosine_convert_fusion = (bf16[1500,512]{1,0:T(8,128)(2,1)}, bf16[1500,512]{1,0:T(8,128)(2,1)}, bf16[1500,512]{1,0:T(8,128)(2,1)}, bf16[1500,512]{1,0:T(8,128)(2...) fusion(s32[1500]{0:T(1024)S(1)} %get-tuple-element.56, ...), kind=kLoop, calls=%fused_computation.75 | loop fusion | flops 73728000 | bytes 24620048 | tf_op jit(solution)/shard_map/convert
  149.9 1.4 collective-permute-start.1
  152.0 9.4 %collective-permute-done.1 = bf16[1,1,16,12000]{3,2,1,0:T(8,128)(2,1)S(1)} collective-permute-done((bf16[1,1,16,12000]{3,2,1,0:T(8,128)(2,1)}, bf16[1,1,16,12000]{3,2,1,0:T(8,128)(2,1)S(1)}, u32[]{:S(2)}, u32[]{:S(2)}) %collective-permute-start.1) | collective-permute-done | bytes 384032 | tf_op jit(solution)/shard_map/ppermute | solution.py:122
  162.8 10.0 %collective-permute-done.2 = bf16[1,1,16,12000]{3,2,1,0:T(8,128)(2,1)S(1)} collective-permute-done((bf16[1,1,16,12000]{3,2,1,0:T(8,128)(2,1)}, bf16[1,1,16,12000]{3,2,1,0:T(8,128)(2,1)S(1)}, u32[]{:S(2)}, u32[]{:S(2)}) %collective-permute-start.2) | collective-permute-done | bytes 384032 | tf_op jit(solution)/shard_map/ppermute | solution.py:122
  173.6 10.3 %collective-permute-done.3 = bf16[1,1,16,12000]{3,2,1,0:T(8,128)(2,1)S(1)} collective-permute-done((bf16[1,1,16,12000]{3,2,1,0:T(8,128)(2,1)}, bf16[1,1,16,12000]{3,2,1,0:T(8,128)(2,1)S(1)}, u32[]{:S(2)}, u32[]{:S(2)}) %collective-permute-start.3) | collective-permute-done | bytes 384032 | tf_op jit(solution)/shard_map/ppermute | solution.py:122
  184.7 10.0 %collective-permute-done.4 = bf16[1,1,16,12000]{3,2,1,0:T(8,128)(2,1)S(1)} collective-permute-done((bf16[1,1,16,12000]{3,2,1,0:T(8,128)(2,1)}, bf16[1,1,16,12000]{3,2,1,0:T(8,128)(2,1)S(1)}, u32[]{:S(2)}, u32[]{:S(2)}) %collective-permute-start.4) | collective-permute-done | bytes 384032 | tf_op jit(solution)/shard_map/ppermute | solution.py:122
  194.7 1.2 collective-permute-start.5
  196.7 9.3 %collective-permute-done.5 = bf16[1,1,16,12000]{3,2,1,0:T(8,128)(2,1)S(1)} collective-permute-done((bf16[1,1,16,12000]{3,2,1,0:T(8,128)(2,1)S(1)}, bf16[1,1,16,12000]{3,2,1,0:T(8,128)(2,1)S(1)}, u32[]{:S(2)}, u32[]{:S(2)}) %collective-permute-start.5) | collective-permute-done | bytes 384032 | tf_op jit(solution)/shard_map/ppermute | solution.py:122
  207.4 10.1 %collective-permute-done.6 = bf16[1,1,16,12000]{3,2,1,0:T(8,128)(2,1)S(1)} collective-permute-done((bf16[1,1,16,12000]{3,2,1,0:T(8,128)(2,1)S(1)}, bf16[1,1,16,12000]{3,2,1,0:T(8,128)(2,1)S(1)}, u32[]{:S(2)}, u32[]{:S(2)}) %collective-permute-start.6) | collective-permute-done | bytes 384032 | tf_op jit(solution)/shard_map/ppermute | solution.py:122
  217.6 3.3 collective-permute-start.7
  221.6 16.1 %collective-permute-done.7 = bf16[1,1,16,12000]{3,2,1,0:T(8,128)(2,1)S(1)} collective-permute-done((bf16[1,1,16,12000]{3,2,1,0:T(8,128)(2,1)S(1)}, bf16[1,1,16,12000]{3,2,1,0:T(8,128)(2,1)S(1)}, u32[]{:S(2)}, u32[]{:S(2)}) %collective-permute-start.7) | collective-permute-done | bytes 384032 | tf_op jit(solution)/shard_map/ppermute | solution.py:122
  238.5 19.2 %collective-permute-done.8 = bf16[1,1,16,12000]{3,2,1,0:T(8,128)(2,1)S(1)} collective-permute-done((bf16[1,1,16,12000]{3,2,1,0:T(8,128)(2,1)S(1)}, bf16[1,1,16,12000]{3,2,1,0:T(8,128)(2,1)S(1)}, u32[]{:S(2)}, u32[]{:S(2)}) %collective-permute-start.8) | collective-permute-done | bytes 384032 | tf_op jit(solution)/shard_map/ppermute | solution.py:122
  258.5 18.4 %collective-permute-done.9 = bf16[1,1,16,12000]{3,2,1,0:T(8,128)(2,1)S(1)} collective-permute-done((bf16[1,1,16,12000]{3,2,1,0:T(8,128)(2,1)S(1)}, bf16[1,1,16,12000]{3,2,1,0:T(8,128)(2,1)S(1)}, u32[]{:S(2)}, u32[]{:S(2)}) %collective-permute-start.9) | collective-permute-done | bytes 384032 | tf_op jit(solution)/shard_map/ppermute | solution.py:122
  277.7 19.6 %collective-permute-done.10 = bf16[1,1,16,12000]{3,2,1,0:T(8,128)(2,1)S(1)} collective-permute-done((bf16[1,1,16,12000]{3,2,1,0:T(8,128)(2,1)S(1)}, bf16[1,1,16,12000]{3,2,1,0:T(8,128)(2,1)S(1)}, u32[]{:S(2)}, u32[]{:S(2)}) %collective-permute-start.10) | collective-permute-done | bytes 384032 | tf_op jit(solution)/shard_map/ppermute | solution.py:122
  301.2 3.5 gather_fusion.1
  322.6 1.7 copy.42
  324.4 47.2 %all-gather.2.cloned.1.call-done = bf16[128,16,2,512]{3,1,2,0:T(8,128)(2,1)} async-done(((bf16[8,16,2,512]{3,1,2,0:T(8,128)(2,1)}), bf16[128,16,2,512]{3,1,2,0:T(8,128)(2,1)}) %all-gather.2.cloned.1.call-update) | async-done | bytes 4194320 | tf_op jit(solution)/shard_map/all_gather | solution.py:135
  371.6 9.1 %copy.41 = bf16[512,2,16,128]{3,2,1,0:T(8,128)(2,1)} copy(bf16[512,2,16,128]{0,2,1,3:T(8,128)(2,1)} %bitcast.92) | data formatting | bytes 8388608 | tf_op jit(solution)/shard_map/transpose | solution.py:61
  380.7 2.5 slice_negate_fusion
  383.2 2.4 maximum_bitcast_fusion
  385.6 9.1 %copy.43 = bf16[512,2,16,128]{3,2,1,0:T(8,128)(2,1)} copy(bf16[512,2,16,128]{0,2,1,3:T(8,128)(2,1)} %maximum_bitcast_fusion) | data formatting | bytes 8388608 | tf_op jit(solution)/shard_map/transpose | solution.py:63
  394.7 3.5 convolution_bitcast_fusion.1
  398.3 1.3 convolution_bitcast_fusion
  399.9 4.6 %copy.45 = bf16[512,8,2,128]{3,2,1,0:T(2,128)(2,1)} copy(bf16[512,8,2,128]{3,1,0,2:T(8,128)(2,1)S(1)} %fusion.4) | data formatting | bytes 4194304 | tf_op jit(solution)/shard_map/convert_element_type | solution.py:70
  (142 shorter events, 38.1 us)
Async XLA Ops:
  6.5 5.3 %copy-start.25 = (s32[8,16]{1,0:T(8,128)S(1)}, s32[8,16]{1,0:T(8,128)}, u32[]{:S(2)}) copy-start(s32[8,16]{1,0:T(8,128)} %param.7) | copy-start | bytes 1540
  6.5 365.0 %all-gather.2.cloned.1.call-start = ((), (), s32[]{:S(2)}) async-start(), calls=%async_computation | async-start | bytes 4456448 | tf_op jit(solution)/shard_map/all_gather | solution.py:135
  22.6 14.4 %copy-start.26 = (s32[128]{0:T(128)S(1)}, s32[128]{0:T(128)}, u32[]{:S(2)}) copy-start(s32[128]{0:T(128)} %param.9) | copy-start | bytes 1540
  22.6 15.7 %copy-start = (s32[128]{0:T(128)S(1)}, s32[128]{0:T(128)}, u32[]{:S(2)}) copy-start(s32[128]{0:T(128)} %param.8) | copy-start | bytes 1540
  24.7 2.6 copy-start.2
  27.3 273.1 %collective-permute-start.14 = (bf16[1,1,16,12000]{3,2,1,0:T(8,128)(2,1)S(1)}, bf16[1,1,16,12000]{3,2,1,0:T(8,128)(2,1)S(1)}, u32[]{:S(2)}, u32[]{:S(2)}) collective-permute-start(bf16[1,1,16,12000]{3,2,1,0:T(8,128)(2,1)S(1)} %get-tuple-element.8), channel_id=1, source_target_pairs={{0,15},{1,14},{2,13},{3,12},{4,11},{5,10},{6,9},{7,8},{8,7},{9,6},... | collective-permute-start | bytes 1152008 | tf_op jit(solution)/shard_map/ppermute | solution.py:122
  32.8 266.9 %collective-permute-start.13 = (bf16[1,1,16,12000]{3,2,1,0:T(8,128)(2,1)S(1)}, bf16[1,1,16,12000]{3,2,1,0:T(8,128)(2,1)S(1)}, u32[]{:S(2)}, u32[]{:S(2)}) collective-permute-start(bf16[1,1,16,12000]{3,2,1,0:T(8,128)(2,1)S(1)} %get-tuple-element.9), channel_id=1, source_target_pairs={{0,14},{1,15},{2,12},{3,13},{4,10},{5,11},{6,8},{7,9},{8,6},{9,7},... | collective-permute-start | bytes 1152008 | tf_op jit(solution)/shard_map/ppermute | solution.py:122
  33.4 265.5 %collective-permute-start.12 = (bf16[1,1,16,12000]{3,2,1,0:T(8,128)(2,1)S(1)}, bf16[1,1,16,12000]{3,2,1,0:T(8,128)(2,1)S(1)}, u32[]{:S(2)}, u32[]{:S(2)}) collective-permute-start(bf16[1,1,16,12000]{3,2,1,0:T(8,128)(2,1)S(1)} %get-tuple-element.10), channel_id=1, source_target_pairs={{0,13},{1,12},{2,15},{3,14},{4,9},{5,8},{6,11},{7,10},{8,5},{9,4},... | collective-permute-start | bytes 1152008 | tf_op jit(solution)/shard_map/ppermute | solution.py:122
  36.6 261.5 %collective-permute-start.11 = (bf16[1,1,16,12000]{3,2,1,0:T(8,128)(2,1)S(1)}, bf16[1,1,16,12000]{3,2,1,0:T(8,128)(2,1)S(1)}, u32[]{:S(2)}, u32[]{:S(2)}) collective-permute-start(bf16[1,1,16,12000]{3,2,1,0:T(8,128)(2,1)S(1)} %get-tuple-element.11), channel_id=1, source_target_pairs={{0,12},{1,13},{2,14},{3,15},{4,8},{5,9},{6,10},{7,11},{8,4},{9,5},... | collective-permute-start | bytes 1152008 | tf_op jit(solution)/shard_map/ppermute | solution.py:122
  36.9 112.9 %collective-permute-start = (bf16[1,1,16,12000]{3,2,1,0:T(8,128)(2,1)}, bf16[1,1,16,12000]{3,2,1,0:T(8,128)(2,1)S(1)}, u32[]{:S(2)}, u32[]{:S(2)}) collective-permute-start(bf16[1,1,16,12000]{3,2,1,0:T(8,128)(2,1)} %get-tuple-element.22), channel_id=1, source_target_pairs={{0,1},{1,0},{2,3},{3,2},{4,5},{5,4},{6,7},{7,6},{8,9},{9,8},{10,11... | collective-permute-start | bytes 1152008 | tf_op jit(solution)/shard_map/ppermute | solution.py:122
  149.8 44.9 %copy-start.24 = (bf16[1,1,16,12000]{3,2,1,0:T(8,128)(2,1)S(1)}, bf16[1,1,16,12000]{3,2,1,0:T(8,128)(2,1)}, u32[]{:S(2)}) copy-start(bf16[1,1,16,12000]{3,2,1,0:T(8,128)(2,1)} %get-tuple-element.17) | copy-start | bytes 1152004
  149.8 56.2 %copy-start.23 = (bf16[1,1,16,12000]{3,2,1,0:T(8,128)(2,1)S(1)}, bf16[1,1,16,12000]{3,2,1,0:T(8,128)(2,1)}, u32[]{:S(2)}) copy-start(bf16[1,1,16,12000]{3,2,1,0:T(8,128)(2,1)} %get-tuple-element.16) | copy-start | bytes 1152004
  149.8 67.8 %copy-start.22 = (bf16[1,1,16,12000]{3,2,1,0:T(8,128)(2,1)S(1)}, bf16[1,1,16,12000]{3,2,1,0:T(8,128)(2,1)}, u32[]{:S(2)}) copy-start(bf16[1,1,16,12000]{3,2,1,0:T(8,128)(2,1)} %get-tuple-element.15) | copy-start | bytes 1152004
  149.8 87.9 %copy-start.21 = (bf16[1,1,16,12000]{3,2,1,0:T(8,128)(2,1)S(1)}, bf16[1,1,16,12000]{3,2,1,0:T(8,128)(2,1)}, u32[]{:S(2)}) copy-start(bf16[1,1,16,12000]{3,2,1,0:T(8,128)(2,1)} %get-tuple-element.14) | copy-start | bytes 1152004
  149.9 11.5 %collective-permute-start.1 = (bf16[1,1,16,12000]{3,2,1,0:T(8,128)(2,1)}, bf16[1,1,16,12000]{3,2,1,0:T(8,128)(2,1)S(1)}, u32[]{:S(2)}, u32[]{:S(2)}) collective-permute-start(bf16[1,1,16,12000]{3,2,1,0:T(8,128)(2,1)} %get-tuple-element.21), channel_id=1, source_target_pairs={{0,2},{1,3},{2,0},{3,1},{4,6},{5,7},{6,4},{7,5},{8,10},{9,11},{10,... | collective-permute-start | bytes 1152008 | tf_op jit(solution)/shard_map/ppermute | solution.py:122
  151.2 106.5 %copy-start.20 = (bf16[1,1,16,12000]{3,2,1,0:T(8,128)(2,1)S(1)}, bf16[1,1,16,12000]{3,2,1,0:T(8,128)(2,1)}, u32[]{:S(2)}) copy-start(bf16[1,1,16,12000]{3,2,1,0:T(8,128)(2,1)} %get-tuple-element.13) | copy-start | bytes 1152004
  161.4 115.6 %copy-start.19 = (bf16[1,1,16,12000]{3,2,1,0:T(8,128)(2,1)S(1)}, bf16[1,1,16,12000]{3,2,1,0:T(8,128)(2,1)}, u32[]{:S(2)}) copy-start(bf16[1,1,16,12000]{3,2,1,0:T(8,128)(2,1)} %get-tuple-element.12) | copy-start | bytes 1152004
  161.4 11.4 %collective-permute-start.2 = (bf16[1,1,16,12000]{3,2,1,0:T(8,128)(2,1)}, bf16[1,1,16,12000]{3,2,1,0:T(8,128)(2,1)S(1)}, u32[]{:S(2)}, u32[]{:S(2)}) collective-permute-start(bf16[1,1,16,12000]{3,2,1,0:T(8,128)(2,1)} %get-tuple-element.20), channel_id=1, source_target_pairs={{0,3},{1,2},{2,1},{3,0},{4,7},{5,6},{6,5},{7,4},{8,11},{9,10},{10,... | collective-permute-start | bytes 1152008 | tf_op jit(solution)/shard_map/ppermute | solution.py:122
  172.8 11.1 %collective-permute-start.3 = (bf16[1,1,16,12000]{3,2,1,0:T(8,128)(2,1)}, bf16[1,1,16,12000]{3,2,1,0:T(8,128)(2,1)S(1)}, u32[]{:S(2)}, u32[]{:S(2)}) collective-permute-start(bf16[1,1,16,12000]{3,2,1,0:T(8,128)(2,1)} %get-tuple-element.19), channel_id=1, source_target_pairs={{0,4},{1,5},{2,6},{3,7},{4,0},{5,1},{6,2},{7,3},{8,12},{9,13},{10,... | collective-permute-start | bytes 1152008 | tf_op jit(solution)/shard_map/ppermute | solution.py:122
  183.9 10.8 %collective-permute-start.4 = (bf16[1,1,16,12000]{3,2,1,0:T(8,128)(2,1)}, bf16[1,1,16,12000]{3,2,1,0:T(8,128)(2,1)S(1)}, u32[]{:S(2)}, u32[]{:S(2)}) collective-permute-start(bf16[1,1,16,12000]{3,2,1,0:T(8,128)(2,1)} %get-tuple-element.18), channel_id=1, source_target_pairs={{0,5},{1,4},{2,7},{3,6},{4,1},{5,0},{6,3},{7,2},{8,13},{9,12},{10,... | collective-permute-start | bytes 1152008 | tf_op jit(solution)/shard_map/ppermute | solution.py:122
  194.7 11.2 %collective-permute-start.5 = (bf16[1,1,16,12000]{3,2,1,0:T(8,128)(2,1)S(1)}, bf16[1,1,16,12000]{3,2,1,0:T(8,128)(2,1)S(1)}, u32[]{:S(2)}, u32[]{:S(2)}) collective-permute-start(bf16[1,1,16,12000]{3,2,1,0:T(8,128)(2,1)S(1)} %copy-done.24), channel_id=1, source_target_pairs={{0,6},{1,7},{2,4},{3,5},{4,2},{5,3},{6,0},{7,1},{8,14},{9,15},{10,... | collective-permute-start | bytes 1152008 | tf_op jit(solution)/shard_map/ppermute | solution.py:122
  206.0 11.6 %collective-permute-start.6 = (bf16[1,1,16,12000]{3,2,1,0:T(8,128)(2,1)S(1)}, bf16[1,1,16,12000]{3,2,1,0:T(8,128)(2,1)S(1)}, u32[]{:S(2)}, u32[]{:S(2)}) collective-permute-start(bf16[1,1,16,12000]{3,2,1,0:T(8,128)(2,1)S(1)} %copy-done.23), channel_id=1, source_target_pairs={{0,7},{1,6},{2,5},{3,4},{4,3},{5,2},{6,1},{7,0},{8,15},{9,14},{10,... | collective-permute-start | bytes 1152008 | tf_op jit(solution)/shard_map/ppermute | solution.py:122
  217.6 20.2 %collective-permute-start.7 = (bf16[1,1,16,12000]{3,2,1,0:T(8,128)(2,1)S(1)}, bf16[1,1,16,12000]{3,2,1,0:T(8,128)(2,1)S(1)}, u32[]{:S(2)}, u32[]{:S(2)}) collective-permute-start(bf16[1,1,16,12000]{3,2,1,0:T(8,128)(2,1)S(1)} %copy-done.22), channel_id=1, source_target_pairs={{0,8},{1,9},{2,10},{3,11},{4,12},{5,13},{6,14},{7,15},{8,0},{9,1},... | collective-permute-start | bytes 1152008 | tf_op jit(solution)/shard_map/ppermute | solution.py:122
  237.7 20.0 %collective-permute-start.8 = (bf16[1,1,16,12000]{3,2,1,0:T(8,128)(2,1)S(1)}, bf16[1,1,16,12000]{3,2,1,0:T(8,128)(2,1)S(1)}, u32[]{:S(2)}, u32[]{:S(2)}) collective-permute-start(bf16[1,1,16,12000]{3,2,1,0:T(8,128)(2,1)S(1)} %copy-done.21), channel_id=1, source_target_pairs={{0,9},{1,8},{2,11},{3,10},{4,13},{5,12},{6,15},{7,14},{8,1},{9,0},... | collective-permute-start | bytes 1152008 | tf_op jit(solution)/shard_map/ppermute | solution.py:122
  257.7 19.2 %collective-permute-start.9 = (bf16[1,1,16,12000]{3,2,1,0:T(8,128)(2,1)S(1)}, bf16[1,1,16,12000]{3,2,1,0:T(8,128)(2,1)S(1)}, u32[]{:S(2)}, u32[]{:S(2)}) collective-permute-start(bf16[1,1,16,12000]{3,2,1,0:T(8,128)(2,1)S(1)} %copy-done.20), channel_id=1, source_target_pairs={{0,10},{1,11},{2,8},{3,9},{4,14},{5,15},{6,12},{7,13},{8,2},{9,3},... | collective-permute-start | bytes 1152008 | tf_op jit(solution)/shard_map/ppermute | solution.py:122
  276.9 20.4 %collective-permute-start.10 = (bf16[1,1,16,12000]{3,2,1,0:T(8,128)(2,1)S(1)}, bf16[1,1,16,12000]{3,2,1,0:T(8,128)(2,1)S(1)}, u32[]{:S(2)}, u32[]{:S(2)}) collective-permute-start(bf16[1,1,16,12000]{3,2,1,0:T(8,128)(2,1)S(1)} %copy-done.19), channel_id=1, source_target_pairs={{0,11},{1,10},{2,9},{3,8},{4,15},{5,14},{6,13},{7,12},{8,3},{9,2},... | collective-permute-start | bytes 1152008 | tf_op jit(solution)/shard_map/ppermute | solution.py:122
  306.6 1.9 copy-start.16
  308.4 1.9 copy-start.14
  310.3 1.9 copy-start.12
  312.2 1.9 copy-start.10
  314.0 1.9 copy-start.8
  394.7 3.5 copy-start.1
  (11 other events, 16.7 us)
Sparse Core Ops, SparseCore 0:
  322.8 48.7 all-gather.1
